TPU v7x, 512 devices: a whole 4x8x8 slice. The times are simulated.
512 devices in a mesh: grp: 32 (over x, y), tp: 16 (over z, core).
Axes of the slice: x: 4, y: 8, z: 8, core: 2. Of those that a mesh axis runs over, the one named last changes fastest.
Arguments:
- patches: bfloat16 [16384, 1664], P('grp'), may hold values from -6 to 6
- patch_image: int32 [16384], P('grp'), may hold values from 0 to 4095, as said below
- vis_gain: float32 [1664], replicated, may hold values from 0.25 to 1.75
- vis_bias: float32 [1664], replicated, may hold values from -3 to 3
- vis_qkv: bfloat16 [3, 1664, 1664], P(None, None, 'tp'), may hold values from -2 to 2
- vis_out: bfloat16 [1664, 1664], P('tp'), may hold values from -0.15625 to 0.15625
- merge_weight: bfloat16 [4, 1664, 1024], P(None, 'tp'), may hold values from -0.078125 to 0.078125
- positions: int32 [4096], P('grp'), may hold values from 0 to 12287, as said below
- text: bfloat16 [8192, 1024], P('grp'), may hold values from -6 to 6
- dec_gain: float32 [1024], replicated, may hold values from 0.25 to 1.75
- dec_bias: float32 [1024], replicated, may hold values from -3 to 3
- dec_qkv: bfloat16 [3, 1024, 1024], P(None, None, 'tp'), may hold values from -2 to 2
Outputs:
- dec_attn: bfloat16 [12288, 1024], P('grp', 'tp')
Inputs may be any that keep to these rules, and one draw needn't show every extreme that they name: `patch_image`: each aligned run of four patches belongs to one image. Groups 2j and 2j+1 are partners: the last image of group 2j continues as the first image of group 2j+1; no other image is shared between groups. All positions are distinct; each group's block of 384 positions holds exactly 128 of them; the 128 merged rows of one group put at most 8 positions into any one group's block.
All inputs are finite; a program needn't handle non-finite values.
Results may differ from a plain program's by a relative error of at most 0.025.
Values may be sent and summed in bfloat16 or wider, within the bound.
No kernel may reach another device: no remote copies, remote signals or barrier semaphores. Data moves between devices by JAX's collectives and lax.ppermute only.
A program may use at most 128 MiB of HBM per device.

v0:
```python
import jax
import jax.numpy as jnp
from jax import lax
from jax.sharding import PartitionSpec as P

HD = 104
DH = 64
layer_eps = 1e-05


def swapped(value, axis, stride):
    return lax.ppermute(value, axis, [(i, i ^ 1 << stride) for i in range(lax.axis_size(axis))])


def normalize(values, gain, bias):
    mean = jnp.mean(values, axis=-1, keepdims=True)
    centred = values - mean
    spread = jnp.mean(centred * centred, axis=-1, keepdims=True)
    return centred * lax.rsqrt(spread + layer_eps) * gain + bias


def body(
    patches,
    patch_image,
    vis_gain,
    vis_bias,
    vis_qkv,
    vis_out,
    merge_weight,
    positions,
    text,
    dec_gain,
    dec_bias,
    dec_qkv,
):
    rows = patches.shape[0]
    heads = vis_qkv.shape[2] // HD
    patches_f = patches.astype(jnp.float32)
    normed = normalize(patches_f, vis_gain, vis_bias).astype(jnp.bfloat16)
    proj = jnp.einsum("pd,sde->spe", normed, vis_qkv, preferred_element_type=jnp.float32).astype(
        jnp.bfloat16
    )
    query = proj[0].reshape(rows, heads, HD)
    partner_kv, partner_ids = swapped((proj[1:], patch_image), "grp", 0)
    both_kv = jnp.concatenate([proj[1:], partner_kv], axis=1)
    both_ids = jnp.concatenate([patch_image, partner_ids], axis=0)
    keys = both_kv[0].reshape(2 * rows, heads, HD)
    values = both_kv[1].reshape(2 * rows, heads, HD)
    scores = jnp.einsum("phe,khe->hpk", query, keys, preferred_element_type=jnp.float32) * HD ** (
        -0.5
    )
    same = patch_image[:, None] == both_ids[None, :]
    top = jnp.max(jnp.where(same, scores, -1e30), axis=2, keepdims=True)
    expo = jnp.where(same, jnp.exp(scores - top), 0.0)
    weights = (expo / jnp.sum(expo, axis=2, keepdims=True)).astype(jnp.bfloat16)
    attended = jnp.einsum(
        "hpk,khe->phe", weights, values, preferred_element_type=jnp.float32
    ).astype(jnp.bfloat16)
    attended = attended.reshape(rows, heads * HD)
    width = patches.shape[1] // lax.axis_size("tp")
    mixed = lax.psum_scatter(
        lax.dot_general(
            vis_out, attended, (((0,), (1,)), ((), ())), preferred_element_type=jnp.float32
        ).astype(jnp.bfloat16),
        "tp",
        scatter_dimension=0,
        tiled=True,
    ).astype(jnp.float32)
    own_cols = lax.dynamic_slice_in_dim(patches_f, lax.axis_index("tp") * width, width, 1)
    visual = (mixed + own_cols.T).astype(jnp.bfloat16)
    windows = visual.reshape(width, rows // 4, 4)
    partial_rows = jnp.einsum(
        "cmk,kce->me", windows, merge_weight, preferred_element_type=jnp.float32
    )
    groups = lax.axis_size("grp")
    here = lax.axis_index("grp")
    merged_count = rows // 4
    text_count = text.shape[0]
    tok = text_count + merged_count
    cap = merged_count // min(groups, 16)
    target = positions // tok
    member = (target[:, None] == jnp.arange(groups, dtype=jnp.int32)[None, :]).astype(jnp.int32)
    rank = jnp.sum(jnp.cumsum(member, axis=0) * member, axis=1) - 1
    slot = target * cap + rank
    select = slot[None, :] == jnp.arange(groups * cap, dtype=jnp.int32)[:, None]
    select_bf = select.astype(jnp.bfloat16)
    bucket_pos = jnp.sum(jnp.where(select, positions[None, :] + 1, 0), axis=1) - 1
    merged = lax.psum(partial_rows.astype(jnp.bfloat16), "tp")
    packed = jnp.dot(select_bf, merged, preferred_element_type=jnp.float32).astype(jnp.bfloat16)
    got_rows, got_pos = (
        lax.all_to_all(packed, "grp", split_axis=0, concat_axis=0, tiled=True),
        lax.all_to_all(bucket_pos, "grp", split_axis=0, concat_axis=0, tiled=True),
    )
    local_pos = got_pos - here * tok
    place = jnp.arange(tok, dtype=jnp.int32)
    landing = (local_pos[None, :] == place[:, None]) & (got_pos[None, :] >= 0)
    image_here = jnp.any(landing, axis=1).astype(jnp.int32)
    text_index = place - (jnp.cumsum(image_here) - image_here)
    text_pick = (image_here[:, None] == 0) & (
        text_index[:, None] == jnp.arange(text_count, dtype=jnp.int32)[None, :]
    )
    prompt = jnp.dot(landing.astype(jnp.bfloat16), got_rows, preferred_element_type=jnp.float32)
    prompt = prompt + jnp.dot(
        text_pick.astype(jnp.bfloat16), text, preferred_element_type=jnp.float32
    )
    dnorm = normalize(prompt, dec_gain, dec_bias).astype(jnp.bfloat16)
    dproj = jnp.einsum("td,sde->ste", dnorm, dec_qkv, preferred_element_type=jnp.float32).astype(
        jnp.bfloat16
    )
    dheads = dec_qkv.shape[2] // DH
    dquery = dproj[0].reshape(tok, dheads, DH)
    query_pos = here * tok + place
    best = jnp.full((dheads, tok), -1e30, jnp.float32)
    key_rows = lax.all_gather(dproj[1], "grp", axis=0, tiled=True).reshape(-1, dheads, DH)
    value_rows = lax.all_gather(dproj[2], "grp", axis=0, tiled=True).reshape(-1, dheads, DH)
    key_pos = jnp.arange(key_rows.shape[0], dtype=jnp.int32)
    score = jnp.einsum(
        "the,rhe->htr", dquery, key_rows, preferred_element_type=jnp.float32
    ) * DH ** (-0.5)
    allowed = key_pos[None, :] <= query_pos[:, None]
    new_best = jnp.maximum(best, jnp.max(jnp.where(allowed[None], score, -1e30), axis=2))
    expo_d = jnp.where(allowed[None], jnp.exp(score - new_best[:, :, None]), 0.0)
    total = jnp.sum(expo_d, axis=2)
    acc = jnp.einsum(
        "htr,rhe->hte", expo_d.astype(jnp.bfloat16), value_rows, preferred_element_type=jnp.float32
    )
    best, total, acc = (new_best, total, acc)
    result = acc / total[:, :, None]
    return result.transpose(1, 0, 2).reshape(tok, dheads * DH).astype(jnp.bfloat16)


def solution(mesh):
    in_specs = (
        P("grp", None),
        P("grp"),
        P(),
        P(),
        P(None, None, "tp"),
        P("tp", None),
        P(None, "tp", None),
        P("grp"),
        P("grp", None),
        P(),
        P(),
        P(None, None, "tp"),
    )
    out_specs = P("grp", "tp")
    return jax.shard_map(body, mesh=mesh, in_specs=in_specs, out_specs=out_specs, check_vma=False)
```

profile of v0, /device:TPU:8, one launch (start us, length us, event | category | flops | bytes accessed | tf_op | source)
XLA Modules:
  0.0 415.6 jit_solution(2915710087922539153)
XLA Ops:
  6.5 0.0 copy-start
  6.5 0.0 reduce-scatter.4.cloned.1.call-start
  6.6 1.9 convert_reduce_fusion
  8.5 0.1 copy-done.1
  8.6 0.6 multiply_reduce_fusion
  9.2 0.0 copy-start.4
  9.2 1.0 fusion.6
  10.3 7.7 %collective-permute-start = (bf16[2,512,104]{1,2,0:T(8,128)(2,1)S(1)}, bf16[2,512,104]{1,2,0:T(8,128)(2,1)S(1)}, u32[]{:S(2)}, u32[]{:S(2)}) collective-permute-start(bf16[2,512,104]{1,2,0:T(8,128)(2,1)S(1)} %slice.38), channel_id=1, source_target_pairs={{0,16},{16,0},{32,48},{48,32},{64,80},{80,64},{96,112},{112,96},{1... | collective-permute-start | bytes 638984 | tf_op jit(solution)/shard_map/ppermute | solution.py:12
  18.1 1.9 collective-permute-start.1
  20.0 3.6 collective-permute-done.1
  23.6 0.0 collective-permute-done
  23.6 0.6 fusion.5
  24.2 1.4 copy-done.2
  25.5 0.7 fusion.13
  26.2 4.3 %fusion.4 = bf16[1664,512]{0,1:T(8,128)(2,1)} fusion(bf16[104,1664]{1,0:T(8,128)(2,1)S(1)} %copy-done.6, f32[512,1024]{1,0:T(8,128)} %copy-done.2, f32[512]{0:T(512)S(1)} %fusion.13, f32[512]{0:T(512)S(1)} %get-tuple-element.11, s32[1024]{0:T(1024)S(1)} %pad_add_fusion, s32[512]{0:T(512)S(1)} %copy-done.4, bf16[2,512,104]{1,2,0:T(8,128)(2,1)S(1)} %slice.38, ...), kind=kOutput, calls=%fused_computation.10 | convolution fusion | flops 290738176 | bytes 4583424 | tf_op jit(solution)/shard_map/dot_general | solution.py:62
  30.5 3.6 copy.17
  34.1 0.0 reduce-scatter.4.cloned.1.call-update
  34.1 0.0 all-reduce.2.cloned.1.call-start
  34.2 0.0 copy-start.11
  34.2 2.0 convert_element_type.82
  36.2 0.0 copy-done.11
  36.2 0.1 fusion.64
  36.3 0.2 reduce_window_sum.30
  36.4 0.2 select_reduce_fusion.2
  36.6 0.1 select_reduce_fusion.1
  36.8 59.7 %reduce-scatter.4.cloned.1.call-done = bf16[104,512]{1,0:T(8,128)(2,1)} async-done(((bf16[1664,512]{1,0:T(8,128)(2,1)}), bf16[104,512]{1,0:T(8,128)(2,1)}) %reduce-scatter.4.cloned.1.call-update) | async-done | bytes 106512
  96.5 1.0 copy.18
  97.5 1.2 fusion.49
  98.7 2.2 fusion.15
  100.9 0.0 all-reduce.2.cloned.1.call-update
  100.9 0.0 copy-start.3
  100.9 0.7 sub.80
  101.6 9.9 %all-to-all-start = ((s32[32,8,1]{1,2,0:T(1,128)}), s32[32,8,1]{1,2,0:T(1,128)S(1)}, u32[]{:S(2)}, u32[]{:S(2)}) async-start(s32[32,8,1]{1,2,0:T(1,128)} %bitcast), calls=%async_computation | async-start | bytes 32768 | tf_op jit(solution)/shard_map/all_to_all | solution.py:92
  111.5 102.0 %all-reduce.2.cloned.1.call-done = bf16[128,1024]{1,0:T(8,128)(2,1)} async-done(((bf16[128,1024]{1,0:T(8,128)(2,1)}), bf16[128,1024]{1,0:T(8,128)(2,1)}) %all-reduce.2.cloned.1.call-update) | async-done | bytes 262160 | tf_op jit(solution)/shard_map/psum | solution.py:88
  213.5 2.0 fusion.14
  215.5 0.0 all-to-all-done
  215.5 9.8 %all-to-all-start.1 = ((bf16[32,8,1024]{2,1,0:T(8,128)(2,1)}), bf16[32,8,1024]{2,1,0:T(8,128)(2,1)S(1)}, u32[]{:S(2)}, u32[]{:S(2)}) async-start(bf16[32,8,1024]{2,1,0:T(8,128)(2,1)} %fusion.14), calls=%async_computation.1 | async-start | bytes 1048576 | tf_op jit(solution)/shard_map/all_to_all | solution.py:91
  225.4 0.0 all-gather.5.cloned.1.call-start
  225.5 0.1 sub.83
  225.6 0.1 compare_reduce_fusion
  225.6 0.1 ge.16
  225.7 0.2 fusion.45
  225.9 0.3 reduce-window.9
  226.2 0.1 slice.33
  226.3 0.1 slice_reduce_fusion
  226.4 0.1 fusion.65
  226.5 16.5 %all-to-all-done.1 = bf16[32,8,1024]{2,1,0:T(8,128)(2,1)S(1)} async-done(((bf16[32,8,1024]{2,1,0:T(8,128)(2,1)}), bf16[32,8,1024]{2,1,0:T(8,128)(2,1)S(1)}, u32[]{:S(2)}, u32[]{:S(2)}) %all-to-all-start.1) | async-done | bytes 524320 | tf_op jit(solution)/shard_map/all_to_all | solution.py:91
  243.0 0.4 fusion.42
  243.4 0.0 copy-start.5
  243.4 0.0 copy-start.9
  243.4 0.0 copy-start.10
  243.4 0.5 fusion.75
  244.0 0.3 multiply_reduce_fusion.1
  244.3 0.1 copy-done.5
  244.4 0.5 fusion.37
  245.0 0.6 fusion.74
  245.6 0.0 all-gather.5.cloned.1.call-update
  245.7 0.2 all-gather.7.cloned.1.call-start
  245.9 0.3 all-gather.7.cloned.1.call-update
  246.3 71.2 %all-gather.5.cloned.1.call-done = bf16[1,12288,64]{1,2,0:T(8,128)(2,1)} async-done(((bf16[1,384,64]{1,2,0:T(8,128)(2,1)}), bf16[1,12288,64]{1,2,0:T(8,128)(2,1)}) %all-gather.5.cloned.1.call-update) | async-done | bytes 1572880 | tf_op jit(solution)/shard_map/all_gather | solution.py:114
  317.4 9.3 %select_reduce_fusion = (f32[384]{0:T(512)S(1)}, f32[384,12288]{1,0:T(8,128)}) fusion(s32[384]{0:T(512)S(1)} %iota_add_fusion, bf16[1,12288,64]{1,2,0:T(8,128)(2,1)} %all-gather.5.cloned.1.call-done, bf16[3,384,64]{1,2,0:T(8,128)(2,1)S(1)} %convert_bitcast_fusion.1), kind=kOutput, calls=%fused_computation.1 | convolution fusion | flops 622853760 | bytes 20499968 | tf_op jit(solution)/shard_map/the,rhe->htr/dot_general | solution.py:117
  326.7 11.1 %fusion = f32[384]{0:T(512)S(1)} fusion(f32[384,12288]{1,0:T(8,128)} %get-tuple-element.16, f32[384]{0:T(512)S(1)} %broadcast_maximum_fusion, s32[384]{0:T(512)S(1)} %iota_add_fusion), kind=kLoop, calls=%fused_computation.4 | loop fusion | flops 18873984 | bytes 18878976 | tf_op jit(solution)/shard_map/reduce_sum | solution.py:123
  337.8 60.2 %all-gather.7.cloned.1.call-done = bf16[1,12288,64]{1,2,0:T(8,128)(2,1)} async-done(((bf16[1,384,64]{1,2,0:T(8,128)(2,1)}), bf16[1,12288,64]{1,2,0:T(8,128)(2,1)}) %all-gather.7.cloned.1.call-update) | async-done | bytes 1572880 | tf_op jit(solution)/shard_map/all_gather | solution.py:115
  398.0 11.1 %fusion.22 = bf16[384,64]{0,1:T(8,128)(2,1)} fusion(bf16[1,12288,64]{1,2,0:T(8,128)(2,1)} %all-gather.7.cloned.1.call-done, f32[384,12288]{1,0:T(8,128)} %get-tuple-element.16, f32[384]{0:T(512)S(1)} %broadcast_maximum_fusion, s32[384]{0:T(512)S(1)} %iota_add_fusion, f32[384]{0:T(512)S(1)} %fusion), kind=kOutput, calls=%fused_computation.34 | convolution fusion | flops 622903296 | bytes 20500992 | tf_op jit(solution)/shard_map/htr,rhe->hte/dot_general | solution.py:124
  (29 shorter events, 0.3 us)
Async XLA Ops:
  6.5 2.6 copy-start
  6.5 2.1 copy-start.1
  6.5 2.7 copy-start.8
  6.5 2.7 copy-start.7
  6.5 89.9 %reduce-scatter.4.cloned.1.call-start = ((), (), s32[]{:S(2)}) async-start(), calls=%async_computation.6 | async-start | bytes 1810432
  9.2 8.9 %copy-start.4 = (s32[512]{0:T(512)S(1)}, s32[512]{0:T(512)}, u32[]{:S(2)}) copy-start(s32[512]{0:T(512)} %param.13) | copy-start | bytes 6148
  10.3 13.2 %collective-permute-start = (bf16[2,512,104]{1,2,0:T(8,128)(2,1)S(1)}, bf16[2,512,104]{1,2,0:T(8,128)(2,1)S(1)}, u32[]{:S(2)}, u32[]{:S(2)}) collective-permute-start(bf16[2,512,104]{1,2,0:T(8,128)(2,1)S(1)} %slice.38), channel_id=1, source_target_pairs={{0,16},{16,0},{32,48},{48,32},{64,80},{80,64},{96,112},{112,96},{1... | collective-permute-start | bytes 638984 | tf_op jit(solution)/shard_map/ppermute | solution.py:12
  18.1 5.5 %collective-permute-start.1 = (s32[512]{0:T(512)S(1)}, s32[512]{0:T(512)S(1)}, u32[]{:S(2)}, u32[]{:S(2)}) collective-permute-start(s32[512]{0:T(512)S(1)} %copy-done.4), channel_id=1, source_target_pairs={{0,16},{16,0},{32,48},{48,32},{64,80},{80,64},{96,112},{112,96},{1... | collective-permute-start | bytes 6152 | tf_op jit(solution)/shard_map/ppermute | solution.py:12
  23.6 2.6 copy-start.6
  24.2 1.4 copy-start.2
  34.1 179.3 %all-reduce.2.cloned.1.call-start = ((), (), s32[]{:S(2)}) async-start(), calls=%async_computation.3 | async-start | bytes 524288 | tf_op jit(solution)/shard_map/psum | solution.py:88
  34.2 2.0 copy-start.11
  100.9 142.5 %copy-start.3 = (bf16[256,1024]{1,0:T(8,128)(2,1)S(1)}, bf16[256,1024]{1,0:T(8,128)(2,1)}, u32[]{:S(2)}) copy-start(bf16[256,1024]{1,0:T(8,128)(2,1)} %param.20) | copy-start | bytes 1572868
  101.6 113.9 %all-to-all-start = ((s32[32,8,1]{1,2,0:T(1,128)}), s32[32,8,1]{1,2,0:T(1,128)S(1)}, u32[]{:S(2)}, u32[]{:S(2)}) async-start(s32[32,8,1]{1,2,0:T(1,128)} %bitcast), calls=%async_computation | async-start | bytes 32768 | tf_op jit(solution)/shard_map/all_to_all | solution.py:92
  215.5 27.5 %all-to-all-start.1 = ((bf16[32,8,1024]{2,1,0:T(8,128)(2,1)}), bf16[32,8,1024]{2,1,0:T(8,128)(2,1)S(1)}, u32[]{:S(2)}, u32[]{:S(2)}) async-start(bf16[32,8,1024]{2,1,0:T(8,128)(2,1)} %fusion.14), calls=%async_computation.1 | async-start | bytes 1048576 | tf_op jit(solution)/shard_map/all_to_all | solution.py:91
  225.4 92.1 %all-gather.5.cloned.1.call-start = ((), (), s32[]{:S(2)}) async-start(), calls=%async_computation.4 | async-start | bytes 1622016 | tf_op jit(solution)/shard_map/all_gather | solution.py:114
  243.4 1.0 copy-start.5
  243.4 1.0 copy-start.9
  243.4 1.0 copy-start.10
  245.7 152.3 %all-gather.7.cloned.1.call-start = ((), (), s32[]{:S(2)}) async-start(), calls=%async_computation.5 | async-start | bytes 1622016 | tf_op jit(solution)/shard_map/all_gather | solution.py:115
Sparse Core Ops, SparseCore 0:
  34.3 62.1 reduce-scatter.3
  101.0 112.4 all-reduce.1
  245.8 71.5 all-gather.4
  320.4 77.5 all-gather.6
where the time goes:
time: 416 us
  waiting for transfers between devices  313 us (75%)
  matrix products  32 us (8%)
  starting transfers between devices  29.7 us (7%)
  other arithmetic  19 us (5%)
  between operations  13.4 us (3%)
  local copies, waits for them, and re-layouts  8.01 us (2%)
    psum x1, waiting for transfers between devices, body(): merged = lax.psum(partial_rows.astype(jnp.bfloat16), 'tp')  102 us
    all_gather x1, waiting for transfers between devices, body(): lax.all_gather(dproj[1], 'grp', axis=0, tiled=True).reshape(-1, dheads, DH)  71.2 us
    all_gather x1, waiting for transfers between devices, body(): lax.all_gather(dproj[2], 'grp', axis=0, tiled=True).reshape(-1, dheads, DH)  60.2 us
    unnamed x5, waiting for transfers between devices  60.1 us
    all_to_all x1, waiting for transfers between devices, body(): lax.all_to_all(packed, 'grp', split_axis=0, concat_axis=0, tiled=True)  16.5 us
    dot_general x1, matrix products, body(): jnp.einsum('htr,rhe->hte', expo_d.astype(jnp.bfloat16), value_rows, prefe...  11.1 us
    reduce_sum x1, other arithmetic, body(): total = jnp.sum(expo_d, axis=2)  11.1 us
    all_to_all x1, starting transfers between devices, body(): lax.all_to_all(bucket_pos, 'grp', split_axis=0, concat_axis=0, tiled=True)  9.88 us
  transfers between devices with their start and end apart: 8, of which 6 were waited for; matrix products, arithmetic and copies ran while one was open for 6% of the time, Pallas kernels for 0%

commit v1 on v0

--- a/solution.py
+++ b/solution.py
@@ -6,6 +6,14 @@
 HD = 104
 DH = 64
 layer_eps = 1e-05
+
+
+def gather_by_exchange(shard, axis, dim):
+    size = lax.axis_size(axis)
+    repeats = [size if d == dim else 1 for d in range(shard.ndim)]
+    return lax.all_to_all(
+        jnp.tile(shard, repeats), axis, split_axis=dim, concat_axis=dim, tiled=True
+    )
 
 
 def swapped(value, axis, stride):
@@ -111,7 +119,7 @@
     dquery = dproj[0].reshape(tok, dheads, DH)
     query_pos = here * tok + place
     best = jnp.full((dheads, tok), -1e30, jnp.float32)
-    key_rows = lax.all_gather(dproj[1], "grp", axis=0, tiled=True).reshape(-1, dheads, DH)
+    key_rows = gather_by_exchange(dproj[1], "grp", 0).reshape(-1, dheads, DH)
     value_rows = lax.all_gather(dproj[2], "grp", axis=0, tiled=True).reshape(-1, dheads, DH)
     key_pos = jnp.arange(key_rows.shape[0], dtype=jnp.int32)
     score = jnp.einsum(

time: 416 us -> 354 us (0.85)
  waiting for transfers between devices: 313 us -> 245 us
  starting transfers between devices: 29.7 us -> 34.5 us
    all_gather x1 -> x0, waiting for transfers between devices: 71.2 us -> none  [body(): lax.all_gather(dproj[1], 'grp', axis=0, tiled=True).reshape(-1, dheads, DH)]
    all_to_all x0 -> x1, waiting for transfers between devices: none -> 39 us  [gather_by_exchange(): lax.all_to_all(jnp.tile(shard, repeats), axis, split_axis=dim, concat_axi...]
    all_gather x1, waiting for transfers between devices: 60.2 us -> 24.1 us  [body(): lax.all_gather(dproj[2], 'grp', axis=0, tiled=True).reshape(-1, dheads, DH)]
    all_to_all x0 -> x1, starting transfers between devices: none -> 4.86 us  [gather_by_exchange(): lax.all_to_all(jnp.tile(shard, repeats), axis, split_axis=dim, concat_axi...]
    unnamed x5 -> x4, waiting for transfers between devices: 60.1 us -> 60.2 us
  transfers between devices with their start and end apart: 8 -> 8, of which waited for: 6 -> 6; matrix products, arithmetic and copies ran while one was open for 6% -> 7% of each run, Pallas kernels for 0% -> 0%
where the time goes in v1:
time: 354 us; the launch traced here: 353 us
  waiting for transfers between devices  245 us (69%)
  starting transfers between devices  34.5 us (10%)
  matrix products  31 us (9%)
  other arithmetic  19 us (5%)
  between operations  13.4 us (4%)
  local copies, waits for them, and re-layouts  9.56 us (3%)
    psum x1, waiting for transfers between devices, body(): merged = lax.psum(partial_rows.astype(jnp.bfloat16), 'tp')  102 us
    unnamed x4, waiting for transfers between devices  60.2 us
    all_to_all x1, waiting for transfers between devices, gather_by_exchange(): lax.all_to_all(jnp.tile(shard, repeats), axis, split_axis=dim, concat_axi...  39 us
    all_gather x1, waiting for transfers between devices, body(): lax.all_gather(dproj[2], 'grp', axis=0, tiled=True).reshape(-1, dheads, DH)  24.1 us
    all_to_all x1, waiting for transfers between devices, body(): lax.all_to_all(packed, 'grp', split_axis=0, concat_axis=0, tiled=True)  16.6 us
    dot_general x1, matrix products, body(): jnp.einsum('htr,rhe->hte', expo_d.astype(jnp.bfloat16), value_rows, prefe...  11.1 us
    reduce_sum x1, other arithmetic, body(): total = jnp.sum(expo_d, axis=2)  11.1 us
    all_to_all x1, starting transfers between devices, body(): lax.all_to_all(bucket_pos, 'grp', split_axis=0, concat_axis=0, tiled=True)  9.88 us
  transfers between devices with their start and end apart: 8, of which 6 were waited for; matrix products, arithmetic and copies ran while one was open for 7% of the time, Pallas kernels for 0%

profile of v1, /device:TPU:8, one launch (start us, length us, event | category | flops | bytes accessed | tf_op | source)
XLA Modules:
  0.0 352.9 jit_solution(12014397949162417747)
XLA Ops:
  6.5 0.0 reduce-scatter.4.cloned.1.call-start
  6.6 1.9 convert_reduce_fusion
  8.5 0.1 copy-done.1
  8.6 0.6 multiply_reduce_fusion
  9.2 0.0 copy-start.4
  9.2 1.0 fusion.6
  10.3 7.7 %collective-permute-start = (bf16[2,512,104]{1,2,0:T(8,128)(2,1)S(1)}, bf16[2,512,104]{1,2,0:T(8,128)(2,1)S(1)}, u32[]{:S(2)}, u32[]{:S(2)}) collective-permute-start(bf16[2,512,104]{1,2,0:T(8,128)(2,1)S(1)} %slice.38), channel_id=1, source_target_pairs={{0,16},{16,0},{32,48},{48,32},{64,80},{80,64},{96,112},{112,96},{1... | collective-permute-start | bytes 638984 | tf_op jit(solution)/shard_map/ppermute | solution.py:20
  18.1 1.9 collective-permute-start.1
  20.0 3.6 %collective-permute-done.1 = s32[512]{0:T(512)S(1)} collective-permute-done((s32[512]{0:T(512)S(1)}, s32[512]{0:T(512)S(1)}, u32[]{:S(2)}, u32[]{:S(2)}) %collective-permute-start.1) | collective-permute-done | bytes 2080 | tf_op jit(solution)/shard_map/ppermute | solution.py:20
  23.6 0.0 collective-permute-done
  23.6 0.6 fusion.5
  24.2 1.4 copy-done.2
  25.5 0.7 fusion.12
  26.2 4.3 %fusion.4 = bf16[1664,512]{0,1:T(8,128)(2,1)} fusion(bf16[104,1664]{1,0:T(8,128)(2,1)S(1)} %copy-done.6, f32[512,1024]{1,0:T(8,128)} %copy-done.2, f32[512]{0:T(512)S(1)} %fusion.12, f32[512]{0:T(512)S(1)} %get-tuple-element.11, s32[1024]{0:T(1024)S(1)} %pad_add_fusion, s32[512]{0:T(512)S(1)} %copy-done.4, bf16[2,512,104]{1,2,0:T(8,128)(2,1)S(1)} %slice.38, ...), kind=kOutput, calls=%fused_computation.10 | convolution fusion | flops 290738176 | bytes 4583424 | tf_op jit(solution)/shard_map/dot_general | solution.py:70
  30.5 3.6 %copy.23 = bf16[1664,512]{1,0:T(8,128)(2,1)} copy(bf16[1664,512]{0,1:T(8,128)(2,1)} %fusion.4) | data formatting | bytes 3407872
  34.1 0.0 reduce-scatter.4.cloned.1.call-update
  34.1 0.0 all-reduce.2.cloned.1.call-start
  34.2 0.0 copy-start.11
  34.2 2.0 convert_element_type.82
  36.2 0.0 copy-done.11
  36.2 0.1 fusion.63
  36.3 0.2 reduce_window_sum.30
  36.4 0.2 select_reduce_fusion.2
  36.6 0.1 select_reduce_fusion.1
  36.8 59.7 %reduce-scatter.4.cloned.1.call-done = bf16[104,512]{1,0:T(8,128)(2,1)} async-done(((bf16[1664,512]{1,0:T(8,128)(2,1)}), bf16[104,512]{1,0:T(8,128)(2,1)}) %reduce-scatter.4.cloned.1.call-update) | async-done | bytes 106512
  96.5 1.0 copy.24
  97.5 1.2 fusion.48
  98.7 2.2 fusion.14
  100.9 0.0 all-reduce.2.cloned.1.call-update
  100.9 0.0 copy-start.3
  100.9 0.7 sub.80
  101.6 9.9 %all-to-all-start = ((s32[32,8,1]{1,2,0:T(1,128)}), s32[32,8,1]{1,2,0:T(1,128)S(1)}, u32[]{:S(2)}, u32[]{:S(2)}) async-start(s32[32,8,1]{1,2,0:T(1,128)} %bitcast), calls=%async_computation | async-start | bytes 32768 | tf_op jit(solution)/shard_map/all_to_all | solution.py:100
  111.5 102.0 %all-reduce.2.cloned.1.call-done = bf16[128,1024]{1,0:T(8,128)(2,1)} async-done(((bf16[128,1024]{1,0:T(8,128)(2,1)}), bf16[128,1024]{1,0:T(8,128)(2,1)}) %all-reduce.2.cloned.1.call-update) | async-done | bytes 262160 | tf_op jit(solution)/shard_map/psum | solution.py:96
  213.5 2.0 fusion.13
  215.5 0.0 all-to-all-done
  215.5 9.8 %all-to-all-start.1 = ((bf16[32,8,1024]{2,1,0:T(8,128)(2,1)}), bf16[32,8,1024]{2,1,0:T(8,128)(2,1)S(1)}, u32[]{:S(2)}, u32[]{:S(2)}) async-start(bf16[32,8,1024]{2,1,0:T(8,128)(2,1)} %fusion.13), calls=%async_computation.1 | async-start | bytes 1048576 | tf_op jit(solution)/shard_map/all_to_all | solution.py:99
  225.4 0.1 sub.83
  225.5 0.1 compare_reduce_fusion
  225.6 0.1 ge.16
  225.7 0.2 fusion.44
  225.8 0.3 reduce-window.9
  226.1 0.1 slice.33
  226.3 0.1 slice_reduce_fusion
  226.4 0.1 fusion.64
  226.5 16.6 %all-to-all-done.1 = bf16[32,8,1024]{2,1,0:T(8,128)(2,1)S(1)} async-done(((bf16[32,8,1024]{2,1,0:T(8,128)(2,1)}), bf16[32,8,1024]{2,1,0:T(8,128)(2,1)S(1)}, u32[]{:S(2)}, u32[]{:S(2)}) %all-to-all-start.1) | async-done | bytes 524320 | tf_op jit(solution)/shard_map/all_to_all | solution.py:99
  243.0 0.4 fusion.41
  243.4 0.0 copy-start.5
  243.4 0.0 copy-start.9
  243.4 0.0 copy-start.10
  243.4 0.5 fusion.73
  244.0 0.3 multiply_reduce_fusion.1
  244.3 0.1 copy-done.5
  244.4 0.5 fusion.36
  245.0 0.6 slice_bitcast_fusion.2
  245.6 1.4 tile.9
  247.0 4.9 %all-to-all-start.2 = ((bf16[32,384,64]{1,2,0:T(8,128)(2,1)}), bf16[32,384,64]{1,2,0:T(8,128)(2,1)S(1)}, u32[]{:S(2)}, u32[]{:S(2)}) async-start(bf16[32,384,64]{1,2,0:T(8,128)(2,1)} %tile.9), calls=%async_computation.2 | async-start | bytes 3145728 | tf_op jit(solution)/shard_map/all_to_all | solution.py:14
  251.9 0.2 all-gather.3.cloned.1.call-start
  252.1 0.5 all-gather.3.cloned.1.call-update
  252.6 39.0 %all-to-all-done.2 = bf16[32,384,64]{1,2,0:T(8,128)(2,1)S(1)} async-done(((bf16[32,384,64]{1,2,0:T(8,128)(2,1)}), bf16[32,384,64]{1,2,0:T(8,128)(2,1)S(1)}, u32[]{:S(2)}, u32[]{:S(2)}) %all-to-all-start.2) | async-done | bytes 1572896 | tf_op jit(solution)/shard_map/all_to_all | solution.py:14
  291.7 0.2 copy.25
  291.9 8.3 %select_reduce_fusion = (f32[384]{0:T(512)S(1)}, f32[384,12288]{1,0:T(8,128)}) fusion(s32[384]{0:T(512)S(1)} %iota_add_fusion, bf16[12288,64]{0,1:T(8,128)(2,1)S(1)} %bitcast.81, bf16[3,384,64]{1,2,0:T(8,128)(2,1)S(1)} %convert_bitcast_fusion.1), kind=kOutput, calls=%fused_computation.1 | convolution fusion | flops 622853760 | bytes 20499968 | tf_op jit(solution)/shard_map/the,rhe->htr/dot_general | solution.py:125
  300.2 11.1 %fusion = f32[384]{0:T(512)S(1)} fusion(f32[384,12288]{1,0:T(8,128)} %get-tuple-element.16, f32[384]{0:T(512)S(1)} %broadcast_maximum_fusion, s32[384]{0:T(512)S(1)} %iota_add_fusion), kind=kLoop, calls=%fused_computation.4 | loop fusion | flops 18873984 | bytes 18878976 | tf_op jit(solution)/shard_map/reduce_sum | solution.py:131
  311.2 24.1 %all-gather.3.cloned.1.call-done = bf16[1,12288,64]{1,2,0:T(8,128)(2,1)} async-done(((bf16[1,384,64]{1,2,0:T(8,128)(2,1)}), bf16[1,12288,64]{1,2,0:T(8,128)(2,1)}) %all-gather.3.cloned.1.call-update) | async-done | bytes 1572880 | tf_op jit(solution)/shard_map/all_gather | solution.py:123
  335.3 11.1 %fusion.21 = bf16[384,64]{0,1:T(8,128)(2,1)} fusion(bf16[1,12288,64]{1,2,0:T(8,128)(2,1)} %all-gather.3.cloned.1.call-done, f32[384,12288]{1,0:T(8,128)} %get-tuple-element.16, f32[384]{0:T(512)S(1)} %broadcast_maximum_fusion, s32[384]{0:T(512)S(1)} %iota_add_fusion, f32[384]{0:T(512)S(1)} %fusion), kind=kOutput, calls=%fused_computation.33 | convolution fusion | flops 622903296 | bytes 20500992 | tf_op jit(solution)/shard_map/htr,rhe->hte/dot_general | solution.py:132
  (30 shorter events, 0.3 us)
Async XLA Ops:
  6.5 2.6 copy-start
  6.5 2.1 copy-start.1
  6.5 2.7 copy-start.8
  6.5 2.7 copy-start.7
  6.5 89.9 %reduce-scatter.4.cloned.1.call-start = ((), (), s32[]{:S(2)}) async-start(), calls=%async_computation.6 | async-start | bytes 1810432
  9.2 8.9 %copy-start.4 = (s32[512]{0:T(512)S(1)}, s32[512]{0:T(512)}, u32[]{:S(2)}) copy-start(s32[512]{0:T(512)} %param.13) | copy-start | bytes 6148
  10.3 13.2 %collective-permute-start = (bf16[2,512,104]{1,2,0:T(8,128)(2,1)S(1)}, bf16[2,512,104]{1,2,0:T(8,128)(2,1)S(1)}, u32[]{:S(2)}, u32[]{:S(2)}) collective-permute-start(bf16[2,512,104]{1,2,0:T(8,128)(2,1)S(1)} %slice.38), channel_id=1, source_target_pairs={{0,16},{16,0},{32,48},{48,32},{64,80},{80,64},{96,112},{112,96},{1... | collective-permute-start | bytes 638984 | tf_op jit(solution)/shard_map/ppermute | solution.py:20
  18.1 5.5 %collective-permute-start.1 = (s32[512]{0:T(512)S(1)}, s32[512]{0:T(512)S(1)}, u32[]{:S(2)}, u32[]{:S(2)}) collective-permute-start(s32[512]{0:T(512)S(1)} %copy-done.4), channel_id=1, source_target_pairs={{0,16},{16,0},{32,48},{48,32},{64,80},{80,64},{96,112},{112,96},{1... | collective-permute-start | bytes 6152 | tf_op jit(solution)/shard_map/ppermute | solution.py:20
  23.6 2.6 copy-start.6
  24.2 1.4 copy-start.2
  34.1 179.3 %all-reduce.2.cloned.1.call-start = ((), (), s32[]{:S(2)}) async-start(), calls=%async_computation.4 | async-start | bytes 524288 | tf_op jit(solution)/shard_map/psum | solution.py:96
  34.2 2.0 copy-start.11
  100.9 142.5 %copy-start.3 = (bf16[256,1024]{1,0:T(8,128)(2,1)S(1)}, bf16[256,1024]{1,0:T(8,128)(2,1)}, u32[]{:S(2)}) copy-start(bf16[256,1024]{1,0:T(8,128)(2,1)} %param.20) | copy-start | bytes 1572868
  101.6 113.9 %all-to-all-start = ((s32[32,8,1]{1,2,0:T(1,128)}), s32[32,8,1]{1,2,0:T(1,128)S(1)}, u32[]{:S(2)}, u32[]{:S(2)}) async-start(s32[32,8,1]{1,2,0:T(1,128)} %bitcast), calls=%async_computation | async-start | bytes 32768 | tf_op jit(solution)/shard_map/all_to_all | solution.py:100
  215.5 27.5 %all-to-all-start.1 = ((bf16[32,8,1024]{2,1,0:T(8,128)(2,1)}), bf16[32,8,1024]{2,1,0:T(8,128)(2,1)S(1)}, u32[]{:S(2)}, u32[]{:S(2)}) async-start(bf16[32,8,1024]{2,1,0:T(8,128)(2,1)} %fusion.13), calls=%async_computation.1 | async-start | bytes 1048576 | tf_op jit(solution)/shard_map/all_to_all | solution.py:99
  243.4 1.0 copy-start.5
  243.4 1.0 copy-start.9
  243.4 1.0 copy-start.10
  247.0 44.7 %all-to-all-start.2 = ((bf16[32,384,64]{1,2,0:T(8,128)(2,1)}), bf16[32,384,64]{1,2,0:T(8,128)(2,1)S(1)}, u32[]{:S(2)}, u32[]{:S(2)}) async-start(bf16[32,384,64]{1,2,0:T(8,128)(2,1)} %tile.9), calls=%async_computation.2 | async-start | bytes 3145728 | tf_op jit(solution)/shard_map/all_to_all | solution.py:14
  251.9 83.4 %all-gather.3.cloned.1.call-start = ((), (), s32[]{:S(2)}) async-start(), calls=%async_computation.5 | async-start | bytes 1622016 | tf_op jit(solution)/shard_map/all_gather | solution.py:123
Sparse Core Ops, SparseCore 0:
  34.3 62.1 reduce-scatter.3
  101.0 112.4 all-reduce.1
  255.8 79.4 all-gather.2
